TPU v7x, 32 devices: a whole 2x2x4 slice. The times are simulated.
32 devices in a mesh: groups: 2 (over y), chan: 4 (over z), tm: 4 (over x, core).
Axes of the slice: x: 2, y: 2, z: 4, core: 2. Of those that a mesh axis runs over, the one named last changes fastest.
Arguments:
- raw: bfloat16 [8192, 2048], P(('groups', 'chan'), 'tm'), parts along dimension 0, may hold values from -20 to 20
- send_blocks: int32 [4, 4, 4, 1], P('chan', 'tm'), may hold values from 0 to 1, as said below
- pair_count: int32 [4, 4, 4], P('chan', 'tm'), may hold values from 0 to 1, as said below
Outputs:
- xspec: bfloat16 [8, 4, 4, 1, 2, 2, 128, 128], P(('groups', 'chan'), 'tm'), parts along dimension 0
There are 2 independent parts, one for each index of `groups`. A program takes and returns all parts, laid end to end along the dimension named above; an argument that names none is the same for every part. Nothing has to cross between parts.
Inputs may be any that keep to these rules, and one draw needn't show every extreme that they name: Each list send_blocks[p, t, c, :] names 1 distinct local blocks of device (p, t). pair_count[c, t, c] is 0; pair_count[c, t, p] is 1 where p and c differ by one; in every index t of tm some owner has 1 from every other source.
All inputs are finite; a program needn't handle non-finite values.
Results may differ from a plain program's by a relative error of at most 0.0066.
Values may be sent and summed in bfloat16 or wider, within the bound.
No kernel may reach another device: no remote copies, remote signals or barrier semaphores. Data moves between devices by JAX's collectives and lax.ppermute only.
A program may use at most 192 MiB of HBM per device.

v0:
```python
import math
import jax
import jax.numpy as jnp
import numpy as np
from jax import lax
from jax.sharding import PartitionSpec as P

BLOCK = 128
NT = 2048
F0 = 128
NBAND = 512
SUBW = 64
RAD = 15


def sinc_value(arg):
    if arg == 0:
        return 1.0
    return math.sin(math.pi * arg) / (math.pi * arg)


def filter_taps():
    low = F0 / NT
    high = (F0 + NBAND) / NT
    taps = []
    for offset in range(-RAD, RAD + 1):
        value = 2.0 * high * sinc_value(2.0 * high * offset) - 2.0 * low * sinc_value(
            2.0 * low * offset
        )
        value = value * (0.5 + 0.5 * math.cos(math.pi * offset / (RAD + 1)))
        taps.append(value)
    return taps


def dft_table():
    samples = np.arange(NT)[:, None]
    freqs = np.arange(F0, F0 + NBAND)[None, :]
    phase = samples * freqs % NT
    angle = 2.0 * np.pi * phase / NT
    return np.concatenate([np.cos(angle), -np.sin(angle)], axis=1)


def band_filter(slab):
    taps = filter_taps()
    signal = slab.astype(jnp.float32)
    total = jnp.zeros(signal.shape, jnp.float32)
    for index in range(2 * RAD + 1):
        total = total + jnp.float32(taps[index]) * jnp.roll(signal, index - RAD, axis=1)
    return total.astype(jnp.bfloat16)


def whiten(spectrum):
    rows = spectrum.shape[0]
    real_part = spectrum[:, :NBAND].reshape(rows, NBAND // SUBW, SUBW)
    imag_part = spectrum[:, NBAND:].reshape(rows, NBAND // SUBW, SUBW)
    power = jnp.mean(real_part * real_part + imag_part * imag_part, axis=2, keepdims=True)
    level = 1.0 / jnp.sqrt(power + 1e-06)
    out = jnp.concatenate(
        [(real_part * level).reshape(rows, NBAND), (imag_part * level).reshape(rows, NBAND)], axis=1
    )
    return out.astype(jnp.bfloat16)


def local(raw, send_blocks, pair_count):
    rows = lax.all_to_all(raw, "tm", split_axis=0, concat_axis=1, tiled=True)
    table = jnp.asarray(dft_table(), dtype=jnp.bfloat16)
    spectrum = jnp.dot(band_filter(rows), table, preferred_element_type=jnp.float32)
    blocks = rows.shape[0] // BLOCK
    whitened = whiten(spectrum).reshape(blocks, BLOCK, 2 * NBAND)
    peers = lax.axis_size("chan")
    width = send_blocks.shape[3]
    every, lists_all = (
        lax.all_gather(whitened, "chan", axis=0, tiled=True),
        lax.all_gather(send_blocks.astype(jnp.bfloat16), "chan", axis=0, tiled=True),
    )
    mine = lax.axis_index("chan")
    column = lax.dynamic_index_in_dim(lists_all[:, 0], mine, axis=1, keepdims=False)
    flat_ids = jnp.arange(peers, dtype=jnp.int32)[:, None] * blocks + column.astype(jnp.int32)
    picked = every[flat_ids]
    turned = jnp.concatenate([whitened[..., NBAND:], -whitened[..., :NBAND]], axis=-1)
    paired = jnp.stack([whitened, turned], axis=1)
    result = jnp.einsum("lrif,pkjf->pklrij", paired, picked, preferred_element_type=jnp.float32)
    result = result * (1.0 / math.sqrt(NBAND))
    live = jnp.arange(width, dtype=jnp.int32)[None, :] < pair_count[0, 0][:, None]
    result = jnp.where(live[:, :, None, None, None, None], result, 0.0)
    return result.astype(jnp.bfloat16)[None, None]


def solution(mesh):
    return jax.shard_map(
        local,
        mesh=mesh,
        in_specs=(P(("groups", "chan"), "tm"), P("chan", "tm", None, None), P("chan", "tm", None)),
        out_specs=P(("groups", "chan"), "tm", None, None, None, None, None, None),
        check_vma=False,
    )
```

profile of v0, /device:TPU:0, one launch (start us, length us, event | category | flops | bytes accessed | tf_op | source)
XLA Modules:
  0.0 150.9 jit_solution(17581047669316288742)
XLA Ops:
  6.5 18.7 %all_to_all.13 = bf16[4,256,512]{2,1,0:T(8,128)(2,1)S(1)} all-to-all(bf16[4,256,512]{2,1,0:T(8,128)(2,1)} %bitcast.81), channel_id=1, replica_groups=mesh['groups'=2,'chan'=4,'tm'=4] {'tm'}, dimensions={0} | all-to-all | bytes 2097152 | tf_op jit(solution)/shard_map/all_to_all | solution.py:65
  25.2 1.6 %convert_bitcast_fusion = f32[256,4,512]{2,0,1:T(8,128)} fusion(bf16[4,256,512]{2,1,0:T(8,128)(2,1)S(1)} %all_to_all.13), kind=kLoop, calls=%fused_computation.62 | loop fusion | flops 524288 | bytes 3145728 | tf_op jit(solution)/shard_map/convert_element_type | solution.py:45
  26.8 1.9 %copy.21 = f32[256,4,512]{0,2,1:T(8,128)S(1)} copy(f32[256,4,512]{2,0,1:T(8,128)} %convert_bitcast_fusion) | data formatting | bytes 4194304 | tf_op jit(solution)/shard_map/convert_element_type | solution.py:45
  28.8 2.3 %fusion.76 = (f32[256,2041]{0,1:T(8,128)}, f32[256,2041]{0,1:T(8,128)}) fusion(f32[256,2048]{0,1:T(8,128)S(1)} %bitcast.46), kind=kLoop, calls=%fused_computation.121 | loop fusion | bytes 8359936 | tf_op jit(solution)/shard_map/jit(_roll_static)/slice | solution.py:48
  31.1 2.3 %fusion.78 = (f32[256,2042]{0,1:T(8,128)}, f32[256,2042]{0,1:T(8,128)}) fusion(f32[256,2048]{0,1:T(8,128)S(1)} %bitcast.47), kind=kLoop, calls=%fused_computation.123 | loop fusion | bytes 8364032 | tf_op jit(solution)/shard_map/jit(_roll_static)/slice | solution.py:48
  33.4 2.3 %fusion.80 = (f32[256,2043]{0,1:T(8,128)}, f32[256,2043]{0,1:T(8,128)}) fusion(f32[256,2048]{0,1:T(8,128)S(1)} %bitcast.48), kind=kLoop, calls=%fused_computation.125 | loop fusion | bytes 8368128 | tf_op jit(solution)/shard_map/jit(_roll_static)/slice | solution.py:48
  35.7 2.3 %fusion.82 = (f32[256,2044]{0,1:T(8,128)}, f32[256,2044]{0,1:T(8,128)}) fusion(f32[256,2048]{0,1:T(8,128)S(1)} %bitcast.49), kind=kLoop, calls=%fused_computation.127 | loop fusion | bytes 8372224 | tf_op jit(solution)/shard_map/jit(_roll_static)/slice | solution.py:48
  38.0 2.3 %fusion.84 = (f32[256,2045]{0,1:T(8,128)}, f32[256,2045]{0,1:T(8,128)}) fusion(f32[256,2048]{0,1:T(8,128)S(1)} %bitcast.50), kind=kLoop, calls=%fused_computation.129 | loop fusion | bytes 8376320 | tf_op jit(solution)/shard_map/jit(_roll_static)/slice | solution.py:48
  40.3 2.3 %fusion.86 = (f32[256,2046]{0,1:T(8,128)}, f32[256,2046]{0,1:T(8,128)}) fusion(f32[256,2048]{0,1:T(8,128)S(1)} %bitcast.51), kind=kLoop, calls=%fused_computation.131 | loop fusion | bytes 8380416 | tf_op jit(solution)/shard_map/jit(_roll_static)/slice | solution.py:48
  42.6 2.3 %fusion.88 = (f32[256,2047]{0,1:T(8,128)}, f32[256,2047]{0,1:T(8,128)}) fusion(f32[256,2048]{0,1:T(8,128)S(1)} %bitcast.52), kind=kLoop, calls=%fused_computation.133 | loop fusion | bytes 8384512 | tf_op jit(solution)/shard_map/jit(_roll_static)/slice | solution.py:48
  44.9 2.3 %fusion.62 = (f32[256,2034]{0,1:T(8,128)}, f32[256,2034]{0,1:T(8,128)}) fusion(f32[256,2048]{0,1:T(8,128)S(1)} %bitcast.53), kind=kLoop, calls=%fused_computation.107 | loop fusion | bytes 8331264 | tf_op jit(solution)/shard_map/jit(_roll_static)/slice | solution.py:48
  47.2 2.3 %fusion.64 = (f32[256,2035]{0,1:T(8,128)}, f32[256,2035]{0,1:T(8,128)}) fusion(f32[256,2048]{0,1:T(8,128)S(1)} %bitcast.54), kind=kLoop, calls=%fused_computation.109 | loop fusion | bytes 8335360 | tf_op jit(solution)/shard_map/jit(_roll_static)/slice | solution.py:48
  49.5 2.3 %fusion.66 = (f32[256,2036]{0,1:T(8,128)}, f32[256,2036]{0,1:T(8,128)}) fusion(f32[256,2048]{0,1:T(8,128)S(1)} %bitcast.55), kind=kLoop, calls=%fused_computation.111 | loop fusion | bytes 8339456 | tf_op jit(solution)/shard_map/jit(_roll_static)/slice | solution.py:48
  51.8 2.3 %fusion.68 = (f32[256,2037]{0,1:T(8,128)}, f32[256,2037]{0,1:T(8,128)}) fusion(f32[256,2048]{0,1:T(8,128)S(1)} %bitcast.56), kind=kLoop, calls=%fused_computation.113 | loop fusion | bytes 8343552 | tf_op jit(solution)/shard_map/jit(_roll_static)/slice | solution.py:48
  54.1 2.3 %fusion.70 = (f32[256,2038]{0,1:T(8,128)}, f32[256,2038]{0,1:T(8,128)}) fusion(f32[256,2048]{0,1:T(8,128)S(1)} %bitcast.57), kind=kLoop, calls=%fused_computation.115 | loop fusion | bytes 8347648 | tf_op jit(solution)/shard_map/jit(_roll_static)/slice | solution.py:48
  56.3 2.3 %fusion.72 = (f32[256,2039]{0,1:T(8,128)}, f32[256,2039]{0,1:T(8,128)}) fusion(f32[256,2048]{0,1:T(8,128)S(1)} %bitcast.58), kind=kLoop, calls=%fused_computation.117 | loop fusion | bytes 8351744 | tf_op jit(solution)/shard_map/jit(_roll_static)/slice | solution.py:48
  58.6 2.2 %fusion.74 = (f32[256,2040]{0,1:T(8,128)}, f32[256,2040]{0,1:T(8,128)}) fusion(f32[256,2048]{0,1:T(8,128)S(1)} %bitcast.59), kind=kLoop, calls=%fused_computation.119 | loop fusion | bytes 8355840 | tf_op jit(solution)/shard_map/jit(_roll_static)/slice | solution.py:48
  60.8 2.3 %fusion.60 = (f32[256,2033]{0,1:T(8,128)}, f32[256,2033]{0,1:T(8,128)}) fusion(f32[256,2048]{0,1:T(8,128)S(1)} %bitcast.60), kind=kLoop, calls=%fused_computation.105 | loop fusion | bytes 8327168 | tf_op jit(solution)/shard_map/jit(_roll_static)/slice | solution.py:48
  63.3 27.8 %fusion.40 = f32[256,1024]{1,0:T(8,128)S(1)} fusion(bf16[2048,1024]{1,0:T(8,128)(2,1)} %constant.58.clone, f32[256,2038]{0,1:T(8,128)} %get-tuple-element.26, f32[256,10]{0,1:T(8,128)S(1)} %get-tuple-element.28, f32[256,2037]{0,1:T(8,128)} %get-tuple-element.22, f32[256,11]{0,1:T(8,128)S(1)} %get-tuple-element.24, f32[256,2036]{0,1:T(8,128)} %get-tuple-element.18, ...), kind=kOutput, calls=%fused_computation.74 | convolution fusion | flops 1121976320 | bytes 70254592 | tf_op jit(solution)/shard_map/dot_general | solution.py:67
  91.1 0.1 multiply_add_fusion
  91.2 0.2 copy.22
  91.6 0.2 copy.23
  91.8 0.0 copy-start
  91.8 0.2 multiply_convert_fusion
  92.0 0.9 pad_maximum_fusion
  92.9 0.0 all-gather.2.cloned.1.call-update
  93.0 11.8 %all_gather.7 = bf16[4,1,4,1]{2,3,1,0:T(2,128)(2,1)S(1)} all-gather(bf16[1,1,4,1]{2,3,1,0:T(2,128)(2,1)S(1)} %convert_element_type.49), channel_id=1, replica_groups=mesh['groups'=2,'chan'=4,'tm'=4] {'chan'}, dimensions={0}, use_global_device_ids=true | all-gather | bytes 40 | tf_op jit(solution)/shard_map/all_gather | solution.py:74
  104.8 0.2 convert_reduce_fusion
  105.1 35.0 %all-gather.2.cloned.1.call-done = bf16[8,128,1024]{2,1,0:T(8,128)(2,1)} async-done(((bf16[2,128,1024]{2,1,0:T(8,128)(2,1)}), bf16[8,128,1024]{2,1,0:T(8,128)(2,1)}) %all-gather.2.cloned.1.call-update) | async-done | bytes 2097168 | tf_op jit(solution)/shard_map/all_gather | solution.py:73
  140.1 2.2 %gather_fusion = bf16[4,128,1024]{2,1,0:T(8,128)(2,1)S(1)} fusion(bf16[8,128,1024]{2,1,0:T(8,128)(2,1)} %all-gather.2.cloned.1.call-done, s32[1024]{0:T(1024)S(1)} %pad_clamp_fusion), kind=kCustom, calls=%fused_computation | custom fusion | bytes 2097168 | tf_op jit(solution)/shard_map/gather | solution.py:79
  142.3 0.8 fusion.34
  143.1 1.0 copy.27
  (27 shorter events, 0.3 us)
Async XLA Ops:
  6.5 133.6 %all-gather.2.cloned.1.call-start = ((), (), s32[]{:S(2)}) async-start(), calls=%async_computation.1 | async-start | bytes 2621440 | tf_op jit(solution)/shard_map/all_gather | solution.py:73
  91.8 1.2 copy-start
  91.8 13.3 %copy-start.1 = (s32[1,1,4]{2,1,0:T(1,128)S(1)}, s32[1,1,4]{2,1,0:T(1,128)}, u32[]{:S(2)}) copy-start(s32[1,1,4]{2,1,0:T(1,128)} %param.6) | copy-start | bytes 52
Sparse Core Ops, SparseCore 0:
  93.1 46.9 all-gather.1
where the time goes:
time: 151 us
  local copies, waits for them, and re-layouts  40 us (26%)
  waiting for transfers between devices  35 us (23%)
  blocking collectives  30.5 us (20%)
  matrix products  28.6 us (19%)
  between operations  13.7 us (9%)
  other arithmetic  3.18 us (2%)
    all_gather x1, waiting for transfers between devices, local(): lax.all_gather(whitened, 'chan', axis=0, tiled=True)  35 us
    slice x30, local copies, waits for them, and re-layouts, band_filter(): jnp.roll(signal, index - RAD, axis=1)  34.4 us
    dot_general x1, matrix products, local(): jnp.dot(band_filter(rows), table, preferred_element_type=jnp.float32)  27.8 us
    all_to_all x1, blocking collectives, local(): rows = lax.all_to_all(raw, 'tm', split_axis=0, concat_axis=1, tiled=True)  18.7 us
    all_gather x1, blocking collectives, local(): lax.all_gather(send_blocks.astype(jnp.bfloat16), 'chan', axis=0, tiled=True)  11.8 us
  transfers between devices with their start and end apart: 1, of which 1 were waited for; matrix products, arithmetic and copies ran while one was open for 0% of the time, Pallas kernels for 0%

commit v1 on v0

--- a/solution.py
+++ b/solution.py
@@ -11,6 +11,14 @@
 NBAND = 512
 SUBW = 64
 RAD = 15
+
+
+def _make_joints(a0, array_axis):
+    a0 = jnp.moveaxis(a0, 0, array_axis)
+    upper = a0.shape
+    return a0.reshape(
+        *upper[:array_axis], upper[array_axis] * upper[array_axis + 1], *upper[array_axis + 2 :]
+    )
 
 
 def sinc_value(arg):
@@ -69,8 +77,32 @@
     whitened = whiten(spectrum).reshape(blocks, BLOCK, 2 * NBAND)
     peers = lax.axis_size("chan")
     width = send_blocks.shape[3]
+
+    def pairs_all_extend(my_data, bus_axis, axis_no):
+        workers = lax.axis_size(bus_axis)
+        all_blocks = [(nth, (nth + 1) % workers) for nth in range(workers)]
+        base_arr, next_value = ([], [])
+        stack_in = [(jj, w) for w, jj in all_blocks]
+        h = 0
+        while h < workers - 1:
+            if h % 2 == 0:
+                base_arr.append(
+                    lax.ppermute(base_arr[-1] if base_arr else my_data, bus_axis, all_blocks)
+                )
+            else:
+                block_next = lax.ppermute(
+                    next_value[-1] if next_value else my_data, bus_axis, stack_in
+                )
+                next_value.append(block_next)
+            h += 1
+        t1 = jnp.stack([*base_arr[::-1], my_data, *next_value], axis=0)
+        mid_arr = lax.axis_index(bus_axis)
+        right_arr = mid_arr - len(base_arr)
+        t1 = t1[(jnp.arange(workers) - right_arr) % workers]
+        return _make_joints(t1, axis_no)
+
     every, lists_all = (
-        lax.all_gather(whitened, "chan", axis=0, tiled=True),
+        pairs_all_extend(whitened, "chan", 0),
         lax.all_gather(send_blocks.astype(jnp.bfloat16), "chan", axis=0, tiled=True),
     )
     mine = lax.axis_index("chan")

time: 151 us -> 136 us (0.901)
  waiting for transfers between devices: 35 us -> 20.6 us
  between operations: 13.7 us -> 0.28 us
  blocking collectives: 30.5 us -> 35.6 us
  starting transfers between devices: 0.01 us -> 4.42 us
  local copies, waits for them, and re-layouts: 40 us -> 42.1 us
    all_gather x1 -> x0, waiting for transfers between devices: 35 us -> none  [local(): lax.all_gather(whitened, 'chan', axis=0, tiled=True)]
    ppermute x0 -> x3, waiting for transfers between devices: none -> 20.6 us  [the longest x1 20.6 us: pairs_all_extend(): lax.ppermute(next_value[-1] if next_value else my_data, bus_axis, stack_in)]
    all_gather x1, blocking collectives: 11.8 us -> 16.9 us  [local(): lax.all_gather(send_blocks.astype(jnp.bfloat16), 'chan', axis=0, tiled=True)]
    ppermute x0 -> x3, starting transfers between devices: none -> 4.42 us  [the longest x2 3.92 us: pairs_all_extend(): lax.ppermute(base_arr[-1] if base_arr else my_data, bus_axis, all_blocks)]
    gather x0 -> x1, local copies, waits for them, and re-layouts: none -> 2.04 us  [pairs_all_extend(): t1 = t1[(jnp.arange(workers) - right_arr) % workers]]
  transfers between devices with their start and end apart: 1 -> 3, of which waited for: 1 -> 1; matrix products, arithmetic and copies ran while one was open for 0% -> 0% of each run, Pallas kernels for 0% -> 0%
where the time goes in v1:
time: 136 us; the launch traced here: 135 us
  local copies, waits for them, and re-layouts  42.1 us (31%)
  blocking collectives  35.6 us (26%)
  matrix products  28.7 us (21%)
  waiting for transfers between devices  20.6 us (15%)
  starting transfers between devices  4.42 us (3%)
  other arithmetic  3.65 us (3%)
    slice x30, local copies, waits for them, and re-layouts, band_filter(): jnp.roll(signal, index - RAD, axis=1)  34.5 us
    dot_general x1, matrix products, local(): jnp.dot(band_filter(rows), table, preferred_element_type=jnp.float32)  27.9 us
    ppermute x1, waiting for transfers between devices, pairs_all_extend(): lax.ppermute(next_value[-1] if next_value else my_data, bus_axis, stack_in)  20.6 us
    all_to_all x1, blocking collectives, local(): rows = lax.all_to_all(raw, 'tm', split_axis=0, concat_axis=1, tiled=True)  18.7 us
    all_gather x1, blocking collectives, local(): lax.all_gather(send_blocks.astype(jnp.bfloat16), 'chan', axis=0, tiled=True)  16.9 us
    ppermute x2, starting transfers between devices, pairs_all_extend(): lax.ppermute(base_arr[-1] if base_arr else my_data, bus_axis, all_blocks)  3.92 us
  transfers between devices with their start and end apart: 3, of which 1 were waited for; matrix products, arithmetic and copies ran while one was open for 0% of the time, Pallas kernels for 0%

profile of v1, /device:TPU:0, one launch (start us, length us, event | category | flops | bytes accessed | tf_op | source)
XLA Modules:
  0.0 135.3 jit_solution(7929040753597264441)
XLA Ops:
  0.0 18.7 %all_to_all.13 = bf16[4,256,512]{2,1,0:T(8,128)(2,1)S(1)} all-to-all(bf16[4,256,512]{2,1,0:T(8,128)(2,1)} %bitcast.94), channel_id=1, replica_groups=mesh['groups'=2,'chan'=4,'tm'=4] {'tm'}, dimensions={0} | all-to-all | bytes 2097152 | tf_op jit(solution)/shard_map/all_to_all | solution.py:73
  18.7 1.7 %convert_bitcast_fusion = f32[256,4,512]{2,0,1:T(8,128)} fusion(bf16[4,256,512]{2,1,0:T(8,128)(2,1)S(1)} %all_to_all.13), kind=kLoop, calls=%fused_computation.64 | loop fusion | flops 524288 | bytes 3145728 | tf_op jit(solution)/shard_map/convert_element_type | solution.py:53
  20.3 1.9 %copy.21 = f32[256,4,512]{0,2,1:T(8,128)S(1)} copy(f32[256,4,512]{2,0,1:T(8,128)} %convert_bitcast_fusion) | data formatting | bytes 4194304 | tf_op jit(solution)/shard_map/convert_element_type | solution.py:53
  22.2 2.3 %fusion.78 = (f32[256,2041]{0,1:T(8,128)}, f32[256,2041]{0,1:T(8,128)}) fusion(f32[256,2048]{0,1:T(8,128)S(1)} %bitcast.54), kind=kLoop, calls=%fused_computation.130 | loop fusion | bytes 8359936 | tf_op jit(solution)/shard_map/jit(_roll_static)/slice | solution.py:56
  24.6 2.3 %fusion.80 = (f32[256,2042]{0,1:T(8,128)}, f32[256,2042]{0,1:T(8,128)}) fusion(f32[256,2048]{0,1:T(8,128)S(1)} %bitcast.55), kind=kLoop, calls=%fused_computation.132 | loop fusion | bytes 8364032 | tf_op jit(solution)/shard_map/jit(_roll_static)/slice | solution.py:56
  26.9 2.3 %fusion.82 = (f32[256,2043]{0,1:T(8,128)}, f32[256,2043]{0,1:T(8,128)}) fusion(f32[256,2048]{0,1:T(8,128)S(1)} %bitcast.56), kind=kLoop, calls=%fused_computation.134 | loop fusion | bytes 8368128 | tf_op jit(solution)/shard_map/jit(_roll_static)/slice | solution.py:56
  29.2 2.3 %fusion.84 = (f32[256,2044]{0,1:T(8,128)}, f32[256,2044]{0,1:T(8,128)}) fusion(f32[256,2048]{0,1:T(8,128)S(1)} %bitcast.57), kind=kLoop, calls=%fused_computation.136 | loop fusion | bytes 8372224 | tf_op jit(solution)/shard_map/jit(_roll_static)/slice | solution.py:56
  31.5 2.3 %fusion.86 = (f32[256,2045]{0,1:T(8,128)}, f32[256,2045]{0,1:T(8,128)}) fusion(f32[256,2048]{0,1:T(8,128)S(1)} %bitcast.58), kind=kLoop, calls=%fused_computation.138 | loop fusion | bytes 8376320 | tf_op jit(solution)/shard_map/jit(_roll_static)/slice | solution.py:56
  33.8 2.3 %fusion.88 = (f32[256,2046]{0,1:T(8,128)}, f32[256,2046]{0,1:T(8,128)}) fusion(f32[256,2048]{0,1:T(8,128)S(1)} %bitcast.59), kind=kLoop, calls=%fused_computation.140 | loop fusion | bytes 8380416 | tf_op jit(solution)/shard_map/jit(_roll_static)/slice | solution.py:56
  36.1 2.3 %fusion.90 = (f32[256,2047]{0,1:T(8,128)}, f32[256,2047]{0,1:T(8,128)}) fusion(f32[256,2048]{0,1:T(8,128)S(1)} %bitcast.60), kind=kLoop, calls=%fused_computation.142 | loop fusion | bytes 8384512 | tf_op jit(solution)/shard_map/jit(_roll_static)/slice | solution.py:56
  38.4 2.3 %fusion.64 = (f32[256,2034]{0,1:T(8,128)}, f32[256,2034]{0,1:T(8,128)}) fusion(f32[256,2048]{0,1:T(8,128)S(1)} %bitcast.61), kind=kLoop, calls=%fused_computation.116 | loop fusion | bytes 8331264 | tf_op jit(solution)/shard_map/jit(_roll_static)/slice | solution.py:56
  40.7 2.3 %fusion.66 = (f32[256,2035]{0,1:T(8,128)}, f32[256,2035]{0,1:T(8,128)}) fusion(f32[256,2048]{0,1:T(8,128)S(1)} %bitcast.62), kind=kLoop, calls=%fused_computation.118 | loop fusion | bytes 8335360 | tf_op jit(solution)/shard_map/jit(_roll_static)/slice | solution.py:56
  43.0 2.3 %fusion.68 = (f32[256,2036]{0,1:T(8,128)}, f32[256,2036]{0,1:T(8,128)}) fusion(f32[256,2048]{0,1:T(8,128)S(1)} %bitcast.63), kind=kLoop, calls=%fused_computation.120 | loop fusion | bytes 8339456 | tf_op jit(solution)/shard_map/jit(_roll_static)/slice | solution.py:56
  45.3 2.3 %fusion.70 = (f32[256,2037]{0,1:T(8,128)}, f32[256,2037]{0,1:T(8,128)}) fusion(f32[256,2048]{0,1:T(8,128)S(1)} %bitcast.64), kind=kLoop, calls=%fused_computation.122 | loop fusion | bytes 8343552 | tf_op jit(solution)/shard_map/jit(_roll_static)/slice | solution.py:56
  47.6 2.3 %fusion.72 = (f32[256,2038]{0,1:T(8,128)}, f32[256,2038]{0,1:T(8,128)}) fusion(f32[256,2048]{0,1:T(8,128)S(1)} %bitcast.65), kind=kLoop, calls=%fused_computation.124 | loop fusion | bytes 8347648 | tf_op jit(solution)/shard_map/jit(_roll_static)/slice | solution.py:56
  49.9 2.3 %fusion.74 = (f32[256,2039]{0,1:T(8,128)}, f32[256,2039]{0,1:T(8,128)}) fusion(f32[256,2048]{0,1:T(8,128)S(1)} %bitcast.66), kind=kLoop, calls=%fused_computation.126 | loop fusion | bytes 8351744 | tf_op jit(solution)/shard_map/jit(_roll_static)/slice | solution.py:56
  52.1 2.2 %fusion.76 = (f32[256,2040]{0,1:T(8,128)}, f32[256,2040]{0,1:T(8,128)}) fusion(f32[256,2048]{0,1:T(8,128)S(1)} %bitcast.67), kind=kLoop, calls=%fused_computation.128 | loop fusion | bytes 8355840 | tf_op jit(solution)/shard_map/jit(_roll_static)/slice | solution.py:56
  54.3 2.3 %fusion.62 = (f32[256,2033]{0,1:T(8,128)}, f32[256,2033]{0,1:T(8,128)}) fusion(f32[256,2048]{0,1:T(8,128)S(1)} %bitcast.68), kind=kLoop, calls=%fused_computation.114 | loop fusion | bytes 8327168 | tf_op jit(solution)/shard_map/jit(_roll_static)/slice | solution.py:56
  56.8 27.9 %fusion.40 = f32[256,1024]{1,0:T(8,128)S(1)} fusion(bf16[2048,1024]{1,0:T(8,128)(2,1)} %constant.76.clone, f32[256,2038]{0,1:T(8,128)} %get-tuple-element.26, f32[256,10]{0,1:T(8,128)S(1)} %get-tuple-element.28, f32[256,2037]{0,1:T(8,128)} %get-tuple-element.22, f32[256,11]{0,1:T(8,128)S(1)} %get-tuple-element.24, f32[256,2036]{0,1:T(8,128)} %get-tuple-element.18, ...), kind=kOutput, calls=%fused_computation.76 | convolution fusion | flops 1121976320 | bytes 70254592 | tf_op jit(solution)/shard_map/dot_general | solution.py:75
  84.9 0.2 copy.22
  85.2 0.2 copy.23
  85.8 2.3 %collective-permute-start = (bf16[2,128,1024]{2,1,0:T(8,128)(2,1)S(1)}, bf16[2,128,1024]{2,1,0:T(8,128)(2,1)S(1)}, u32[]{:S(2)}, u32[]{:S(2)}) collective-permute-start(bf16[2,128,1024]{2,1,0:T(8,128)(2,1)S(1)} %get-tuple-element.67), channel_id=1, source_target_pairs={{0,4},{4,8},{8,12},{12,0},{1,5},{5,9},{9,13},{13,1},{2,6},{6,10},{... | collective-permute-start | bytes 1572872 | tf_op jit(solution)/shard_map/ppermute | solution.py:90
  88.1 16.9 %all_gather.3 = bf16[4,1,4,1]{2,3,1,0:T(2,128)(2,1)S(1)} all-gather(bf16[1,1,4,1]{2,3,1,0:T(2,128)(2,1)S(1)} %convert_element_type.56), channel_id=1, replica_groups=mesh['groups'=2,'chan'=4,'tm'=4] {'chan'}, dimensions={0}, use_global_device_ids=true | all-gather | bytes 40 | tf_op jit(solution)/shard_map/all_gather | solution.py:106
  105.0 0.2 convert_reduce_fusion
  105.3 0.5 collective-permute-start.2
  105.8 1.6 %collective-permute-start.1 = (bf16[2,128,1024]{2,1,0:T(8,128)(2,1)S(1)}, bf16[2,128,1024]{2,1,0:T(8,128)(2,1)S(1)}, u32[]{:S(2)}, u32[]{:S(2)}) collective-permute-start(bf16[2,128,1024]{2,1,0:T(8,128)(2,1)S(1)} %collective-permute-done), channel_id=1, source_target_pairs={{0,4},{4,8},{8,12},{12,0},{1,5},{5,9},{9,13},{13,1},{2,6},{6,10},{... | collective-permute-start | bytes 1572872 | tf_op jit(solution)/shard_map/ppermute | solution.py:90
  107.4 20.6 %collective-permute-done.2 = bf16[2,128,1024]{2,1,0:T(8,128)(2,1)S(1)} collective-permute-done((bf16[2,128,1024]{2,1,0:T(8,128)(2,1)S(1)}, bf16[2,128,1024]{2,1,0:T(8,128)(2,1)S(1)}, u32[]{:S(2)}, u32[]{:S(2)}) %collective-permute-start.2) | collective-permute-done | bytes 524320 | tf_op jit(solution)/shard_map/ppermute | solution.py:93
  128.0 1.2 pad_maximum_fusion
  129.3 2.0 %gather_fusion = bf16[4,2,128,1024]{3,2,1,0:T(8,128)(2,1)} fusion(bf16[4,2,128,1024]{3,2,1,0:T(8,128)(2,1)S(1)} %pad_maximum_fusion, s32[1024]{0:T(1024)S(1)} %pad_clamp_fusion.1), kind=kCustom, calls=%fused_computation | custom fusion | bytes 4194320 | tf_op jit(solution)/shard_map/gather | solution.py:101
  131.3 2.2 %gather_fusion.1 = bf16[4,128,1024]{2,1,0:T(8,128)(2,1)S(1)} fusion(bf16[8,128,1024]{2,1,0:T(8,128)(2,1)} %bitcast.85, s32[1024]{0:T(1024)S(1)} %pad_clamp_fusion), kind=kCustom, calls=%fused_computation.1 | custom fusion | bytes 2097168 | tf_op jit(solution)/shard_map/gather | solution.py:111
  133.5 0.7 fusion.34
  134.3 1.0 copy.27
  (36 shorter events, 0.7 us)
Async XLA Ops:
  85.4 2.7 %copy-start.1 = (s32[1,1,4,1]{2,3,1,0:T(1,128)S(1)}, s32[1,1,4,1]{2,3,1,0:T(1,128)}, u32[]{:S(2)}) copy-start(s32[1,1,4,1]{2,3,1,0:T(1,128)} %param.5) | copy-start | bytes 52
  85.4 22.0 %copy-start.2 = (s32[1,1,4]{2,1,0:T(1,128)S(1)}, s32[1,1,4]{2,1,0:T(1,128)}, u32[]{:S(2)}) copy-start(s32[1,1,4]{2,1,0:T(1,128)} %param.6) | copy-start | bytes 52
  85.8 20.0 %collective-permute-start = (bf16[2,128,1024]{2,1,0:T(8,128)(2,1)S(1)}, bf16[2,128,1024]{2,1,0:T(8,128)(2,1)S(1)}, u32[]{:S(2)}, u32[]{:S(2)}) collective-permute-start(bf16[2,128,1024]{2,1,0:T(8,128)(2,1)S(1)} %get-tuple-element.67), channel_id=1, source_target_pairs={{0,4},{4,8},{8,12},{12,0},{1,5},{5,9},{9,13},{13,1},{2,6},{6,10},{... | collective-permute-start | bytes 1572872 | tf_op jit(solution)/shard_map/ppermute | solution.py:90
  105.3 22.7 %collective-permute-start.2 = (bf16[2,128,1024]{2,1,0:T(8,128)(2,1)S(1)}, bf16[2,128,1024]{2,1,0:T(8,128)(2,1)S(1)}, u32[]{:S(2)}, u32[]{:S(2)}) collective-permute-start(bf16[2,128,1024]{2,1,0:T(8,128)(2,1)S(1)} %get-tuple-element.67), channel_id=1, source_target_pairs={{4,0},{8,4},{12,8},{0,12},{5,1},{9,5},{13,9},{1,13},{6,2},{10,6},{... | collective-permute-start | bytes 1572872 | tf_op jit(solution)/shard_map/ppermute | solution.py:93
  105.8 22.2 %copy-start = (bf16[2,128,1024]{2,1,0:T(8,128)(2,1)}, bf16[2,128,1024]{2,1,0:T(8,128)(2,1)S(1)}, u32[]{:S(2)}) copy-start(bf16[2,128,1024]{2,1,0:T(8,128)(2,1)S(1)} %collective-permute-done) | copy-start | bytes 1572868
  105.8 22.2 %collective-permute-start.1 = (bf16[2,128,1024]{2,1,0:T(8,128)(2,1)S(1)}, bf16[2,128,1024]{2,1,0:T(8,128)(2,1)S(1)}, u32[]{:S(2)}, u32[]{:S(2)}) collective-permute-start(bf16[2,128,1024]{2,1,0:T(8,128)(2,1)S(1)} %collective-permute-done), channel_id=1, source_target_pairs={{0,4},{4,8},{8,12},{12,0},{1,5},{5,9},{9,13},{13,1},{2,6},{6,10},{... | collective-permute-start | bytes 1572872 | tf_op jit(solution)/shard_map/ppermute | solution.py:90
